TPU v7x, 32 devices: a whole 2x2x4 slice. The times are simulated.
32 devices in a mesh: blk: 8 (over z, x), cent: 4 (over y, core).
Axes of the slice: x: 2, y: 2, z: 4, core: 2. Of those that a mesh axis runs over, the one named last changes fastest.
Arguments:
- descriptors: bfloat16 [6144, 1024], P('blk'), may hold values from -6 to 6
- landmarks: bfloat16 [4096, 1024], P('blk'), may hold values from -6 to 6
- whitening: bfloat16 [4096, 4096], P('blk', 'cent'), may hold values from -0.09375 to 0.09375
- centroids: bfloat16 [4096, 4096], P('cent'), may hold values from -8 to 8, as said below
Outputs:
- assign: bfloat16 [6144, 4096], P('blk', 'cent')
- new_centroids: float32 [4096, 4096], P('blk', 'cent')
Inputs may be any that keep to these rules, and one draw needn't show every extreme that they name: `centroids`: centroid coordinates.
All inputs are finite; a program needn't handle non-finite values.
Results may differ from a plain program's by a relative error of at most 0.03.
Values may be sent and summed in bfloat16 or wider, within the bound.
No kernel may reach another device: no remote copies, remote signals or barrier semaphores. Data moves between devices by JAX's collectives and lax.ppermute only.
A program may use at most 128 MiB of HBM per device.

v0:
```python
import math

import jax
import jax.numpy as jnp
from jax import lax
from jax.sharding import PartitionSpec as P


def unit_rows(values):
    wide = values.astype(jnp.float32)
    sum_sq = jnp.sum(wide * wide, axis=1, keepdims=True)
    scale = lax.rsqrt(sum_sq + 1e-06)
    return (wide * scale).astype(jnp.bfloat16)


def ring_order(nb):
    if nb % 2:
        return list(range(nb))
    half = nb // 2
    return [2 * i for i in range(half)] + [2 * i + 1 for i in reversed(range(half))]


def run_steps(first, last, step, carry, unroll):
    if unroll:
        for s in range(first, last):
            carry = step(s, carry)
        return carry
    return lax.fori_loop(first, last, step, carry)


def make_per_device(nb, nc):
    ring = ring_order(nb)
    pos_of = [0] * nb
    for i, b in enumerate(ring):
        pos_of[b] = i
    fwd = [(ring[i], ring[(i + 1) % nb]) for i in range(nb)]
    bwd = [(ring[(i + 1) % nb], ring[i]) for i in range(nb)]
    mates = [(c, c ^ 1) for c in range(nc)]
    snake = nb % 2 == 0
    half_nb = nb // 2

    def pos_of_blk(b):
        if not snake:
            return b
        return jnp.where(b % 2 == 0, b // 2, nb - 1 - b // 2)

    def blk_at(i):
        i = i % nb
        if not snake:
            return i
        return jnp.where(i < half_nb, 2 * i, 2 * (nb - 1 - i) + 1)
    unroll = nb <= 8

    def per_device(descriptors, landmarks, whitening, centroids):
        me = lax.axis_index("blk")
        cme = lax.axis_index("cent")
        par = cme % 2
        p = pos_of_blk(me)

        def ring_blk(i):
            return blk_at(i)

        unit_desc = unit_rows(descriptors)
        unit_land = unit_rows(landmarks)
        sharpness = math.sqrt(descriptors.shape[1])
        mw = whitening.shape[0]
        h = mw // 2
        qh = h // 2

        def feat_part(land_rows, w_rows):
            cos = lax.dot_general(
                unit_desc, land_rows, (((1,), (1,)), ((), ())), preferred_element_type=jnp.float32
            )
            kern = jnp.exp(sharpness * cos).astype(jnp.bfloat16)
            return jnp.dot(kern, w_rows, preferred_element_type=jnp.float32)

        la = lax.dynamic_slice_in_dim(unit_land, par * qh, qh, axis=0)
        lb = lax.dynamic_slice_in_dim(unit_land, h + par * qh, qh, axis=0)
        acc = feat_part(unit_land, whitening)

        def mine_first(rows):
            swapped = jnp.concatenate([rows[qh:], rows[:qh]], 0)
            return jnp.where(par == 0, rows, swapped)

        def w_step(s, carry):
            wa, wb, la, lb, acc = carry
            wa = lax.ppermute(wa, "blk", fwd)
            wb = lax.ppermute(wb, "blk", bwd)
            la = lax.ppermute(la, "blk", fwd)
            lb = lax.ppermute(lb, "blk", bwd)
            ta = lax.ppermute(la, "cent", mates)
            tb = lax.ppermute(lb, "cent", mates)
            land = jnp.concatenate([la, ta, lb, tb], 0)
            wrows = jnp.concatenate([wa, wb], 0)
            acc = lax.optimization_barrier(acc + feat_part(land, wrows))
            return wa, wb, la, lb, acc

        carry = (mine_first(whitening[:h]), mine_first(whitening[h:]), la, lb, acc)
        *_, acc = run_steps(1, nb, w_step, carry, unroll)
        feature_cols = acc.astype(jnp.bfloat16)

        cw = feature_cols.shape[1]
        if nc == 4:
            ypair = [(c, c ^ 2) for c in range(nc)]
            nrow = feature_cols.shape[0]
            nchunk = 4 if nrow % 64 == 0 else 1
            step = nrow // nchunk
            ys, fars = [], []
            for j in range(nchunk):
                y_j = lax.ppermute(feature_cols[j * step:(j + 1) * step], "cent", ypair)
                ys.append(y_j)
                fars.append(lax.ppermute(y_j, "cent", mates))
            from_mate = lax.ppermute(feature_cols, "cent", mates)
            pieces = [feature_cols, from_mate, jnp.concatenate(ys, 0), jnp.concatenate(fars, 0)]
            blocks = [cme ^ t for t in range(nc)]
        else:
            pieces = [feature_cols] + [
                lax.ppermute(feature_cols, "cent", [(c, (c + t) % nc) for c in range(nc)])
                for t in range(1, nc)
            ]
            blocks = [(cme - t) % nc for t in range(nc)]
        logits = None
        for piece, blk in zip(pieces, blocks):
            cpart = lax.dynamic_slice_in_dim(centroids, blk * cw, cw, axis=1)
            part = lax.dot_general(
                piece, cpart, (((1,), (1,)), ((), ())), preferred_element_type=jnp.float32
            )
            logits = part if logits is None else logits + part
        features = jnp.concatenate(pieces, axis=1)
        local_top = jnp.max(logits, axis=1)
        local_sum = jnp.sum(jnp.exp(logits - local_top[:, None]), axis=1)
        stats = jnp.stack([local_top, local_sum], 0)
        peers = [stats] + [
            lax.ppermute(stats, "cent", [(c, (c + k) % nc) for c in range(nc)]) for k in range(1, nc)
        ]
        row_top = peers[0][0]
        for st in peers[1:]:
            row_top = jnp.maximum(row_top, st[0])
        row_total = peers[0][1] * jnp.exp(peers[0][0] - row_top)
        for st in peers[1:]:
            row_total = row_total + st[1] * jnp.exp(st[0] - row_top)
        weights = jnp.exp(logits - row_top[:, None])
        assign = (weights / row_total[:, None]).astype(jnp.bfloat16)
        part_counts = jnp.sum(assign.astype(jnp.float32), axis=0)

        rb = features.shape[1] // nb
        rh = rb // 2

        def part_sums(blk, off):
            col = blk * rb + off
            cblk = col // cw
            if nc == 4:
                t = cblk ^ cme
            else:
                t = (cme - cblk) % nc
            cols = lax.dynamic_slice_in_dim(features, t * cw + col % cw, rh, axis=1)
            return lax.optimization_barrier(
                lax.dot_general(
                    cols, assign, (((0,), (0,)), ((), ())), preferred_element_type=jnp.float32
                )
            )

        def r_step(s, carry):
            acc_a, acc_b, cnt_send, cnt = carry
            ra = lax.ppermute(acc_a.astype(jnp.bfloat16), "blk", fwd)
            rbk = lax.ppermute(acc_b.astype(jnp.bfloat16), "blk", bwd)
            cnt_send = lax.ppermute(cnt_send, "blk", fwd)
            pa = part_sums(ring_blk(p - 1 - s), 0)
            pb = part_sums(ring_blk(p + 1 + s), rh)
            return ra.astype(jnp.float32) + pa, rbk.astype(jnp.float32) + pb, cnt_send, cnt + cnt_send

        acc_a = part_sums(ring_blk(p - 1), 0)
        acc_b = part_sums(ring_blk(p + 1), rh)
        acc_a, acc_b, _, counts = run_steps(
            1, nb, r_step, (acc_a, acc_b, part_counts, part_counts), False
        )
        sums = jnp.concatenate([acc_a, acc_b], axis=0)
        return (assign, sums / jnp.maximum(counts, 1.0)[None, :])

    return per_device


def solution(mesh):
    in_specs = (P("blk", None), P("blk", None), P("blk", "cent"), P("cent", None))
    out_specs = (P("blk", "cent"), P("blk", "cent"))
    per_device = make_per_device(mesh.shape["blk"], mesh.shape["cent"])
    return jax.shard_map(
        per_device, mesh=mesh, in_specs=in_specs, out_specs=out_specs, check_vma=False
    )
```

profile of v0, /device:TPU:0, one launch (start us, length us, event | category | flops | bytes accessed | tf_op | source)
XLA Modules:
  0.0 310.4 jit_solution(9315844258484184209)
XLA Ops:
  3.8 3.0 collective-permute-start.5
  9.4 4.8 %collective-permute-done.5 = bf16[128,1024]{1,0:T(8,128)(2,1)} collective-permute-done((bf16[128,1024]{1,0:T(8,128)(2,1)S(1)}, bf16[128,1024]{1,0:T(8,128)(2,1)}, u32[]{:S(2)}, u32[]{:S(2)}) %collective-permute-start.5) | collective-permute-done | bytes 262176 | tf_op jit(solution)/shard_map/ppermute | solution.py:90
  18.7 6.7 %collective-permute-done.8 = bf16[256,1024]{1,0:T(8,128)(2,1)} collective-permute-done((bf16[256,1024]{1,0:T(8,128)(2,1)S(1)}, bf16[256,1024]{1,0:T(8,128)(2,1)}, u32[]{:S(2)}, u32[]{:S(2)}) %collective-permute-start.8) | collective-permute-done | bytes 524320 | tf_op jit(solution)/shard_map/ppermute | solution.py:88
  27.3 3.6 %collective-permute-done.11 = bf16[128,1024]{1,0:T(8,128)(2,1)S(1)} collective-permute-done((bf16[128,1024]{1,0:T(8,128)(2,1)}, bf16[128,1024]{1,0:T(8,128)(2,1)S(1)}, u32[]{:S(2)}, u32[]{:S(2)}) %collective-permute-start.11) | collective-permute-done | bytes 262176 | tf_op jit(solution)/shard_map/ppermute | solution.py:90
  36.3 4.9 %fusion.118 = f32[768,1024]{1,0:T(8,128)} fusion(bf16[512,1024]{1,0:T(8,128)(2,1)S(1)} %copy-done.3, bf16[512,1024]{1,0:T(8,128)(2,1)S(1)} %fusion.9, bf16[768,1024]{1,0:T(8,128)(2,1)} %param.6, f32[768]{0:T(1024)S(1)} %add_rsqrt_fusion), kind=kOutput, calls=%fused_computation.115 | convolution fusion | flops 1613758464 | bytes 6818816 | tf_op jit(solution)/shard_map/dot_general | solution.py:75
  42.8 4.2 %collective-permute-done.17 = bf16[128,1024]{1,0:T(8,128)(2,1)} collective-permute-done((bf16[128,1024]{1,0:T(8,128)(2,1)S(1)}, bf16[128,1024]{1,0:T(8,128)(2,1)}, u32[]{:S(2)}, u32[]{:S(2)}) %collective-permute-start.17) | collective-permute-done | bytes 262176 | tf_op jit(solution)/shard_map/ppermute | solution.py:90
  49.3 6.4 %convolution_add_fusion.6 = f32[768,1024]{1,0:T(8,128)} fusion(f32[768,1024]{1,0:T(8,128)} %fusion.118, bf16[128,1024]{1,0:T(8,128)(2,1)S(1)} %copy-done.7, bf16[128,1024]{1,0:T(8,128)(2,1)} %collective-permute-done.5, bf16[128,1024]{1,0:T(8,128)(2,1)} %collective-permute-done.4, bf16[128,1024]{1,0:T(8,128)(2,1)} %collective-permute-done.3, ...), kind=kOutput, calls=%fused_computation.36 | convolution fusion | flops 1620836352 | bytes 9964544 | tf_op jit(solution)/shard_map/dot_general | solution.py:75
  61.1 5.6 %convolution_add_fusion.5 = f32[768,1024]{1,0:T(8,128)} fusion(f32[768,1024]{1,0:T(8,128)} %convolution_add_fusion.6, bf16[128,1024]{1,0:T(8,128)(2,1)} %collective-permute-done.12, bf16[128,1024]{1,0:T(8,128)(2,1)S(1)} %collective-permute-done.11, bf16[128,1024]{1,0:T(8,128)(2,1)} %collective-permute-done.10, ...), kind=kOutput, calls=%fused_computation.35 | convolution fusion | flops 1620836352 | bytes 9964544 | tf_op jit(solution)/shard_map/dot_general | solution.py:75
  69.0 7.9 %collective-permute-done.20 = bf16[256,1024]{1,0:T(8,128)(2,1)} collective-permute-done((bf16[256,1024]{1,0:T(8,128)(2,1)S(1)}, bf16[256,1024]{1,0:T(8,128)(2,1)}, u32[]{:S(2)}, u32[]{:S(2)}) %collective-permute-start.20) | collective-permute-done | bytes 524320 | tf_op jit(solution)/shard_map/ppermute | solution.py:88
  79.0 5.9 %convolution_add_fusion.4 = f32[768,1024]{1,0:T(8,128)} fusion(f32[768,1024]{1,0:T(8,128)} %convolution_add_fusion.5, bf16[128,1024]{1,0:T(8,128)(2,1)} %copy-done.8, bf16[128,1024]{1,0:T(8,128)(2,1)} %collective-permute-done.17, bf16[128,1024]{1,0:T(8,128)(2,1)} %collective-permute-done.16, bf16[128,1024]{1,0:T(8,128)(2,1)} %collective-permute-done.15, ...), kind=kOutput, calls=%fused_computation.34 | convolution fusion | flops 1620836352 | bytes 9964544 | tf_op jit(solution)/shard_map/dot_general | solution.py:75
  86.7 6.4 %collective-permute-done.26 = bf16[256,1024]{1,0:T(8,128)(2,1)S(1)} collective-permute-done((bf16[256,1024]{1,0:T(8,128)(2,1)}, bf16[256,1024]{1,0:T(8,128)(2,1)S(1)}, u32[]{:S(2)}, u32[]{:S(2)}) %collective-permute-start.26) | collective-permute-done | bytes 524320 | tf_op jit(solution)/shard_map/ppermute | solution.py:88
  95.1 5.7 %convolution_add_fusion.3 = f32[768,1024]{1,0:T(8,128)} fusion(f32[768,1024]{1,0:T(8,128)} %convolution_add_fusion.4, bf16[128,1024]{1,0:T(8,128)(2,1)} %collective-permute-done.24, bf16[128,1024]{1,0:T(8,128)(2,1)} %collective-permute-done.23, bf16[128,1024]{1,0:T(8,128)(2,1)} %collective-permute-done.22, bf16[128,1024]{1,0:T(8,128)(2,1)} %collective-permute-done.21, ...), kind=kOutput, calls=%fused_computation.33 | convolution fusion | flops 1620836352 | bytes 9964544 | tf_op jit(solution)/shard_map/dot_general | solution.py:75
  102.9 5.1 %collective-permute-done.32 = bf16[256,1024]{1,0:T(8,128)(2,1)} collective-permute-done((bf16[256,1024]{1,0:T(8,128)(2,1)S(1)}, bf16[256,1024]{1,0:T(8,128)(2,1)}, u32[]{:S(2)}, u32[]{:S(2)}) %collective-permute-start.32) | collective-permute-done | bytes 524320 | tf_op jit(solution)/shard_map/ppermute | solution.py:88
  110.0 5.9 %convolution_add_fusion.2 = f32[768,1024]{1,0:T(8,128)} fusion(f32[768,1024]{1,0:T(8,128)} %convolution_add_fusion.3, bf16[128,1024]{1,0:T(8,128)(2,1)} %collective-permute-done.30, bf16[128,1024]{1,0:T(8,128)(2,1)} %collective-permute-done.29, bf16[128,1024]{1,0:T(8,128)(2,1)} %collective-permute-done.28, bf16[128,1024]{1,0:T(8,128)(2,1)} %collective-permute-done.27, ...), kind=kOutput, calls=%fused_computation.32 | convolution fusion | flops 1620836352 | bytes 9964544 | tf_op jit(solution)/shard_map/dot_general | solution.py:75
  116.4 7.1 %collective-permute-done.38 = bf16[256,1024]{1,0:T(8,128)(2,1)S(1)} collective-permute-done((bf16[256,1024]{1,0:T(8,128)(2,1)}, bf16[256,1024]{1,0:T(8,128)(2,1)S(1)}, u32[]{:S(2)}, u32[]{:S(2)}) %collective-permute-start.38) | collective-permute-done | bytes 524320 | tf_op jit(solution)/shard_map/ppermute | solution.py:88
  125.5 5.6 %convolution_add_fusion.1 = f32[768,1024]{1,0:T(8,128)} fusion(f32[768,1024]{1,0:T(8,128)} %convolution_add_fusion.2, bf16[128,1024]{1,0:T(8,128)(2,1)} %collective-permute-done.36, bf16[128,1024]{1,0:T(8,128)(2,1)S(1)} %collective-permute-done.35, bf16[128,1024]{1,0:T(8,128)(2,1)} %collective-permute-done.34, ...), kind=kOutput, calls=%fused_computation.31 | convolution fusion | flops 1620836352 | bytes 9964544 | tf_op jit(solution)/shard_map/dot_general | solution.py:75
  131.2 5.2 %collective-permute-done.44 = bf16[256,1024]{1,0:T(8,128)(2,1)} collective-permute-done((bf16[256,1024]{1,0:T(8,128)(2,1)S(1)}, bf16[256,1024]{1,0:T(8,128)(2,1)}, u32[]{:S(2)}, u32[]{:S(2)}) %collective-permute-start.44) | collective-permute-done | bytes 524320 | tf_op jit(solution)/shard_map/ppermute | solution.py:88
  137.5 4.4 %convolution_add_fusion = bf16[768,1024]{1,0:T(8,128)(2,1)S(1)} fusion(f32[768,1024]{1,0:T(8,128)} %convolution_add_fusion.1, bf16[128,1024]{1,0:T(8,128)(2,1)} %collective-permute-done.42, bf16[128,1024]{1,0:T(8,128)(2,1)} %collective-permute-done.41, bf16[128,1024]{1,0:T(8,128)(2,1)} %collective-permute-done.40, ...), kind=kOutput, calls=%fused_computation.30 | convolution fusion | flops 1621622784 | bytes 8391680 | tf_op jit(solution)/shard_map/dot_general | solution.py:75
  146.3 3.7 %fusion.16 = f32[768,1024]{1,0:T(8,128)S(1)} fusion(bf16[768,1024]{1,0:T(8,128)(2,1)S(1)} %convolution_add_fusion, bf16[1024,4096]{1,0:T(8,128)(2,1)} %param.9, s32[]{:T(128)S(6)} %select_n.215), kind=kOutput, calls=%fused_computation.28 | convolution fusion | flops 1610612736 | bytes 6815748 | tf_op jit(solution)/shard_map/dot_general | solution.py:125
  149.9 4.3 %collective-permute-done.46 = bf16[192,1024]{1,0:T(8,128)(2,1)S(1)} collective-permute-done((bf16[192,1024]{1,0:T(8,128)(2,1)S(1)}, bf16[192,1024]{1,0:T(8,128)(2,1)S(1)}, u32[]{:S(2)}, u32[]{:S(2)}) %collective-permute-start.46) | collective-permute-done | bytes 393248 | tf_op jit(solution)/shard_map/ppermute | solution.py:110
  154.3 8.3 %collective-permute-done.47 = bf16[192,1024]{1,0:T(8,128)(2,1)S(1)} collective-permute-done((bf16[192,1024]{1,0:T(8,128)(2,1)S(1)}, bf16[192,1024]{1,0:T(8,128)(2,1)S(1)}, u32[]{:S(2)}, u32[]{:S(2)}) %collective-permute-start.47) | collective-permute-done | bytes 393248 | tf_op jit(solution)/shard_map/ppermute | solution.py:110
  162.7 8.3 %collective-permute-done.48 = bf16[192,1024]{1,0:T(8,128)(2,1)S(1)} collective-permute-done((bf16[192,1024]{1,0:T(8,128)(2,1)S(1)}, bf16[192,1024]{1,0:T(8,128)(2,1)S(1)}, u32[]{:S(2)}, u32[]{:S(2)}) %collective-permute-start.48) | collective-permute-done | bytes 393248 | tf_op jit(solution)/shard_map/ppermute | solution.py:110
  171.2 7.8 %collective-permute-done.49 = bf16[192,1024]{1,0:T(8,128)(2,1)S(1)} collective-permute-done((bf16[192,1024]{1,0:T(8,128)(2,1)S(1)}, bf16[192,1024]{1,0:T(8,128)(2,1)S(1)}, u32[]{:S(2)}, u32[]{:S(2)}) %collective-permute-start.49) | collective-permute-done | bytes 393248 | tf_op jit(solution)/shard_map/ppermute | solution.py:110
  194.9 112.1 %while.22 = (s32[]{:T(128)}, f32[256,1024]{1,0:T(8,128)S(1)}, f32[256,1024]{1,0:T(8,128)}, f32[1024]{0:T(1024)S(1)}, f32[1024]{0:T(1024)S(1)}, /*index=5*/s32[]{...) while((s32[]{:T(128)}, f32[256,1024]{1,0:T(8,128)S(1)}, ...), condition=%wide.region_6.7_spmd, body=%wide.region_5.6_spmd.sunk | while | flops 806880256 | bytes 22844684 | solution.py:28
  202.0 7.9 %collective-permute-done.2 = f32[1024]{0:T(1024)S(1)} collective-permute-done((f32[1024]{0:T(1024)S(1)}, f32[1024]{0:T(1024)S(1)}, u32[]{:S(2)}, u32[]{:S(2)}) %collective-permute-start.2) | collective-permute-done | bytes 4128 | tf_op jit(solution)/shard_map/while/body/eval_jaxpr/ppermute | solution.py:167
  220.5 7.0 %collective-permute-done.2 = f32[1024]{0:T(1024)S(1)} collective-permute-done((f32[1024]{0:T(1024)S(1)}, f32[1024]{0:T(1024)S(1)}, u32[]{:S(2)}, u32[]{:S(2)}) %collective-permute-start.2) | collective-permute-done | bytes 4128 | tf_op jit(solution)/shard_map/while/body/eval_jaxpr/ppermute | solution.py:167
  238.0 6.3 %collective-permute-done.2 = f32[1024]{0:T(1024)S(1)} collective-permute-done((f32[1024]{0:T(1024)S(1)}, f32[1024]{0:T(1024)S(1)}, u32[]{:S(2)}, u32[]{:S(2)}) %collective-permute-start.2) | collective-permute-done | bytes 4128 | tf_op jit(solution)/shard_map/while/body/eval_jaxpr/ppermute | solution.py:167
  254.9 5.4 %collective-permute-done.2 = f32[1024]{0:T(1024)S(1)} collective-permute-done((f32[1024]{0:T(1024)S(1)}, f32[1024]{0:T(1024)S(1)}, u32[]{:S(2)}, u32[]{:S(2)}) %collective-permute-start.2) | collective-permute-done | bytes 4128 | tf_op jit(solution)/shard_map/while/body/eval_jaxpr/ppermute | solution.py:167
  270.9 4.5 %collective-permute-done.2 = f32[1024]{0:T(1024)S(1)} collective-permute-done((f32[1024]{0:T(1024)S(1)}, f32[1024]{0:T(1024)S(1)}, u32[]{:S(2)}, u32[]{:S(2)}) %collective-permute-start.2) | collective-permute-done | bytes 4128 | tf_op jit(solution)/shard_map/while/body/eval_jaxpr/ppermute | solution.py:167
  286.0 3.7 %collective-permute-done.2 = f32[1024]{0:T(1024)S(1)} collective-permute-done((f32[1024]{0:T(1024)S(1)}, f32[1024]{0:T(1024)S(1)}, u32[]{:S(2)}, u32[]{:S(2)}) %collective-permute-start.2) | collective-permute-done | bytes 4128 | tf_op jit(solution)/shard_map/while/body/eval_jaxpr/ppermute | solution.py:167
  300.4 3.1 %collective-permute-done.2 = f32[1024]{0:T(1024)S(1)} collective-permute-done((f32[1024]{0:T(1024)S(1)}, f32[1024]{0:T(1024)S(1)}, u32[]{:S(2)}, u32[]{:S(2)}) %collective-permute-start.2) | collective-permute-done | bytes 4128 | tf_op jit(solution)/shard_map/while/body/eval_jaxpr/ppermute | solution.py:167
  307.0 3.5 %maximum_divide_fusion = f32[512,1024]{1,0:T(8,128)} fusion(f32[256,1024]{1,0:T(8,128)} %get-tuple-element.276, f32[256,1024]{1,0:T(8,128)S(1)} %get-tuple-element.275, f32[1024]{0:T(1024)S(1)} %broadcast_maximum_fusion), kind=kLoop, calls=%fused_computation.21 | loop fusion | flops 1048576 | bytes 4198400 | tf_op jit(solution)/shard_map/div | solution.py:178
  (254 shorter events, 137.0 us)
Async XLA Ops:
  7.3 18.1 %collective-permute-start.8 = (bf16[256,1024]{1,0:T(8,128)(2,1)S(1)}, bf16[256,1024]{1,0:T(8,128)(2,1)}, u32[]{:S(2)}, u32[]{:S(2)}) collective-permute-start(bf16[256,1024]{1,0:T(8,128)(2,1)S(1)} %get-tuple-element.311), channel_id=1, source_target_pairs={{8,0},{16,8},{24,16},{28,24},{20,28},{12,20},{4,12},{0,4},{9,1},{1... | collective-permute-start | bytes 1572872 | tf_op jit(solution)/shard_map/ppermute | solution.py:88
  14.2 20.3 %collective-permute-start.7 = (bf16[256,1024]{1,0:T(8,128)(2,1)S(1)}, bf16[256,1024]{1,0:T(8,128)(2,1)}, u32[]{:S(2)}, u32[]{:S(2)}) collective-permute-start(bf16[256,1024]{1,0:T(8,128)(2,1)S(1)} %get-tuple-element.310), channel_id=1, source_target_pairs={{0,8},{8,16},{16,24},{24,28},{28,20},{20,12},{12,4},{4,0},{1,9},{9... | collective-permute-start | bytes 1572872 | tf_op jit(solution)/shard_map/ppermute | solution.py:87
  16.2 14.7 %collective-permute-start.11 = (bf16[128,1024]{1,0:T(8,128)(2,1)}, bf16[128,1024]{1,0:T(8,128)(2,1)S(1)}, u32[]{:S(2)}, u32[]{:S(2)}) collective-permute-start(bf16[128,1024]{1,0:T(8,128)(2,1)} %collective-permute-done.5), channel_id=1, source_target_pairs={{8,0},{16,8},{24,16},{28,24},{20,28},{12,20},{4,12},{0,4},{9,1},{1... | collective-permute-start | bytes 786440 | tf_op jit(solution)/shard_map/ppermute | solution.py:90
  16.5 17.9 %collective-permute-start.9 = (bf16[128,1024]{1,0:T(8,128)(2,1)}, bf16[128,1024]{1,0:T(8,128)(2,1)}, u32[]{:S(2)}, u32[]{:S(2)}) collective-permute-start(bf16[128,1024]{1,0:T(8,128)(2,1)} %collective-permute-done.3), channel_id=1, source_target_pairs={{0,8},{8,16},{16,24},{24,28},{28,20},{20,12},{12,4},{4,0},{1,9},{9... | collective-permute-start | bytes 786440 | tf_op jit(solution)/shard_map/ppermute | solution.py:89
  25.4 23.5 %collective-permute-start.14 = (bf16[256,1024]{1,0:T(8,128)(2,1)}, bf16[256,1024]{1,0:T(8,128)(2,1)S(1)}, u32[]{:S(2)}, u32[]{:S(2)}) collective-permute-start(bf16[256,1024]{1,0:T(8,128)(2,1)} %collective-permute-done.8), channel_id=1, source_target_pairs={{8,0},{16,8},{24,16},{28,24},{20,28},{12,20},{4,12},{0,4},{9,1},{1... | collective-permute-start | bytes 1572872 | tf_op jit(solution)/shard_map/ppermute | solution.py:88
  30.9 16.1 %collective-permute-start.17 = (bf16[128,1024]{1,0:T(8,128)(2,1)S(1)}, bf16[128,1024]{1,0:T(8,128)(2,1)}, u32[]{:S(2)}, u32[]{:S(2)}) collective-permute-start(bf16[128,1024]{1,0:T(8,128)(2,1)S(1)} %collective-permute-done.11), channel_id=1, source_target_pairs={{8,0},{16,8},{24,16},{28,24},{20,28},{12,20},{4,12},{0,4},{9,1},{1... | collective-permute-start | bytes 786440 | tf_op jit(solution)/shard_map/ppermute | solution.py:90
  41.2 15.0 %collective-permute-start.13 = (bf16[256,1024]{1,0:T(8,128)(2,1)}, bf16[256,1024]{1,0:T(8,128)(2,1)S(1)}, u32[]{:S(2)}, u32[]{:S(2)}) collective-permute-start(bf16[256,1024]{1,0:T(8,128)(2,1)} %collective-permute-done.7), channel_id=1, source_target_pairs={{0,8},{8,16},{16,24},{24,28},{28,20},{20,12},{12,4},{4,0},{1,9},{9... | collective-permute-start | bytes 1572872 | tf_op jit(solution)/shard_map/ppermute | solution.py:87
  57.7 19.2 %collective-permute-start.20 = (bf16[256,1024]{1,0:T(8,128)(2,1)S(1)}, bf16[256,1024]{1,0:T(8,128)(2,1)}, u32[]{:S(2)}, u32[]{:S(2)}) collective-permute-start(bf16[256,1024]{1,0:T(8,128)(2,1)S(1)} %collective-permute-done.14), channel_id=1, source_target_pairs={{8,0},{16,8},{24,16},{28,24},{20,28},{12,20},{4,12},{0,4},{9,1},{1... | collective-permute-start | bytes 1572872 | tf_op jit(solution)/shard_map/ppermute | solution.py:88
  59.3 19.1 %collective-permute-start.19 = (bf16[256,1024]{1,0:T(8,128)(2,1)S(1)}, bf16[256,1024]{1,0:T(8,128)(2,1)S(1)}, u32[]{:S(2)}, u32[]{:S(2)}) collective-permute-start(bf16[256,1024]{1,0:T(8,128)(2,1)S(1)} %collective-permute-done.13), channel_id=1, source_target_pairs={{0,8},{8,16},{16,24},{24,28},{28,20},{20,12},{12,4},{4,0},{1,9},{9... | collective-permute-start | bytes 1572872 | tf_op jit(solution)/shard_map/ppermute | solution.py:87
  66.8 18.0 %collective-permute-start.27 = (bf16[128,1024]{1,0:T(8,128)(2,1)}, bf16[128,1024]{1,0:T(8,128)(2,1)}, u32[]{:S(2)}, u32[]{:S(2)}) collective-permute-start(bf16[128,1024]{1,0:T(8,128)(2,1)} %collective-permute-done.21), channel_id=1, source_target_pairs={{0,8},{8,16},{16,24},{24,28},{28,20},{20,12},{12,4},{4,0},{1,9},{9... | collective-permute-start | bytes 786440 | tf_op jit(solution)/shard_map/ppermute | solution.py:89
  68.6 16.2 %collective-permute-start.30 = (bf16[128,1024]{1,0:T(8,128)(2,1)}, bf16[128,1024]{1,0:T(8,128)(2,1)}, u32[]{:S(2)}, u32[]{:S(2)}) collective-permute-start(bf16[128,1024]{1,0:T(8,128)(2,1)} %collective-permute-done.29), channel_id=1, source_target_pairs={{0,1},{1,0},{2,3},{3,2},{4,5},{5,4},{6,7},{7,6},{8,9},{9,8},{10,11... | collective-permute-start | bytes 786440 | tf_op jit(solution)/shard_map/ppermute | solution.py:92
  68.9 17.6 %collective-permute-start.35 = (bf16[128,1024]{1,0:T(8,128)(2,1)}, bf16[128,1024]{1,0:T(8,128)(2,1)S(1)}, u32[]{:S(2)}, u32[]{:S(2)}) collective-permute-start(bf16[128,1024]{1,0:T(8,128)(2,1)} %collective-permute-done.29), channel_id=1, source_target_pairs={{8,0},{16,8},{24,16},{28,24},{20,28},{12,20},{4,12},{0,4},{9,1},{1... | collective-permute-start | bytes 786440 | tf_op jit(solution)/shard_map/ppermute | solution.py:90
  76.9 16.1 %collective-permute-start.26 = (bf16[256,1024]{1,0:T(8,128)(2,1)}, bf16[256,1024]{1,0:T(8,128)(2,1)S(1)}, u32[]{:S(2)}, u32[]{:S(2)}) collective-permute-start(bf16[256,1024]{1,0:T(8,128)(2,1)} %collective-permute-done.20), channel_id=1, source_target_pairs={{8,0},{16,8},{24,16},{28,24},{20,28},{12,20},{4,12},{0,4},{9,1},{1... | collective-permute-start | bytes 1572872 | tf_op jit(solution)/shard_map/ppermute | solution.py:88
  78.4 16.3 %collective-permute-start.25 = (bf16[256,1024]{1,0:T(8,128)(2,1)S(1)}, bf16[256,1024]{1,0:T(8,128)(2,1)S(1)}, u32[]{:S(2)}, u32[]{:S(2)}) collective-permute-start(bf16[256,1024]{1,0:T(8,128)(2,1)S(1)} %collective-permute-done.19), channel_id=1, source_target_pairs={{0,8},{8,16},{16,24},{24,28},{28,20},{20,12},{12,4},{4,0},{1,9},{9... | collective-permute-start | bytes 1572872 | tf_op jit(solution)/shard_map/ppermute | solution.py:87
  84.8 16.0 %collective-permute-start.28 = (bf16[128,1024]{1,0:T(8,128)(2,1)}, bf16[128,1024]{1,0:T(8,128)(2,1)}, u32[]{:S(2)}, u32[]{:S(2)}) collective-permute-start(bf16[128,1024]{1,0:T(8,128)(2,1)} %collective-permute-done.27), channel_id=1, source_target_pairs={{0,1},{1,0},{2,3},{3,2},{4,5},{5,4},{6,7},{7,6},{8,9},{9,8},{10,11... | collective-permute-start | bytes 786440 | tf_op jit(solution)/shard_map/ppermute | solution.py:91
  84.8 17.6 %collective-permute-start.33 = (bf16[128,1024]{1,0:T(8,128)(2,1)}, bf16[128,1024]{1,0:T(8,128)(2,1)}, u32[]{:S(2)}, u32[]{:S(2)}) collective-permute-start(bf16[128,1024]{1,0:T(8,128)(2,1)} %collective-permute-done.27), channel_id=1, source_target_pairs={{0,8},{8,16},{16,24},{24,28},{28,20},{20,12},{12,4},{4,0},{1,9},{9... | collective-permute-start | bytes 786440 | tf_op jit(solution)/shard_map/ppermute | solution.py:89
  86.5 16.0 %collective-permute-start.36 = (bf16[128,1024]{1,0:T(8,128)(2,1)S(1)}, bf16[128,1024]{1,0:T(8,128)(2,1)}, u32[]{:S(2)}, u32[]{:S(2)}) collective-permute-start(bf16[128,1024]{1,0:T(8,128)(2,1)S(1)} %collective-permute-done.35), channel_id=1, source_target_pairs={{0,1},{1,0},{2,3},{3,2},{4,5},{5,4},{6,7},{7,6},{8,9},{9,8},{10,11... | collective-permute-start | bytes 786440 | tf_op jit(solution)/shard_map/ppermute | solution.py:92
  93.1 14.9 %collective-permute-start.32 = (bf16[256,1024]{1,0:T(8,128)(2,1)S(1)}, bf16[256,1024]{1,0:T(8,128)(2,1)}, u32[]{:S(2)}, u32[]{:S(2)}) collective-permute-start(bf16[256,1024]{1,0:T(8,128)(2,1)S(1)} %collective-permute-done.26), channel_id=1, source_target_pairs={{8,0},{16,8},{24,16},{28,24},{20,28},{12,20},{4,12},{0,4},{9,1},{1... | collective-permute-start | bytes 1572872 | tf_op jit(solution)/shard_map/ppermute | solution.py:88
  94.7 14.9 %collective-permute-start.31 = (bf16[256,1024]{1,0:T(8,128)(2,1)S(1)}, bf16[256,1024]{1,0:T(8,128)(2,1)S(1)}, u32[]{:S(2)}, u32[]{:S(2)}) collective-permute-start(bf16[256,1024]{1,0:T(8,128)(2,1)S(1)} %collective-permute-done.25), channel_id=1, source_target_pairs={{0,8},{8,16},{16,24},{24,28},{28,20},{20,12},{12,4},{4,0},{1,9},{9... | collective-permute-start | bytes 1572872 | tf_op jit(solution)/shard_map/ppermute | solution.py:87
  100.8 15.1 %collective-permute-start.41 = (bf16[128,1024]{1,0:T(8,128)(2,1)S(1)}, bf16[128,1024]{1,0:T(8,128)(2,1)}, u32[]{:S(2)}, u32[]{:S(2)}) collective-permute-start(bf16[128,1024]{1,0:T(8,128)(2,1)S(1)} %collective-permute-done.35), channel_id=1, source_target_pairs={{8,0},{16,8},{24,16},{28,24},{20,28},{12,20},{4,12},{0,4},{9,1},{1... | collective-permute-start | bytes 786440 | tf_op jit(solution)/shard_map/ppermute | solution.py:90
  102.5 23.1 %collective-permute-start.34 = (bf16[128,1024]{1,0:T(8,128)(2,1)}, bf16[128,1024]{1,0:T(8,128)(2,1)}, u32[]{:S(2)}, u32[]{:S(2)}) collective-permute-start(bf16[128,1024]{1,0:T(8,128)(2,1)} %collective-permute-done.33), channel_id=1, source_target_pairs={{0,1},{1,0},{2,3},{3,2},{4,5},{5,4},{6,7},{7,6},{8,9},{9,8},{10,11... | collective-permute-start | bytes 786440 | tf_op jit(solution)/shard_map/ppermute | solution.py:91
  108.0 15.5 %collective-permute-start.38 = (bf16[256,1024]{1,0:T(8,128)(2,1)}, bf16[256,1024]{1,0:T(8,128)(2,1)S(1)}, u32[]{:S(2)}, u32[]{:S(2)}) collective-permute-start(bf16[256,1024]{1,0:T(8,128)(2,1)} %collective-permute-done.32), channel_id=1, source_target_pairs={{8,0},{16,8},{24,16},{28,24},{20,28},{12,20},{4,12},{0,4},{9,1},{1... | collective-permute-start | bytes 1572872 | tf_op jit(solution)/shard_map/ppermute | solution.py:88
  109.6 15.4 %collective-permute-start.37 = (bf16[256,1024]{1,0:T(8,128)(2,1)S(1)}, bf16[256,1024]{1,0:T(8,128)(2,1)S(1)}, u32[]{:S(2)}, u32[]{:S(2)}) collective-permute-start(bf16[256,1024]{1,0:T(8,128)(2,1)S(1)} %collective-permute-done.31), channel_id=1, source_target_pairs={{0,8},{8,16},{16,24},{24,28},{28,20},{20,12},{12,4},{4,0},{1,9},{9... | collective-permute-start | bytes 1572872 | tf_op jit(solution)/shard_map/ppermute | solution.py:87
  115.9 15.3 %collective-permute-start.42 = (bf16[128,1024]{1,0:T(8,128)(2,1)}, bf16[128,1024]{1,0:T(8,128)(2,1)}, u32[]{:S(2)}, u32[]{:S(2)}) collective-permute-start(bf16[128,1024]{1,0:T(8,128)(2,1)} %collective-permute-done.41), channel_id=1, source_target_pairs={{0,1},{1,0},{2,3},{3,2},{4,5},{5,4},{6,7},{7,6},{8,9},{9,8},{10,11... | collective-permute-start | bytes 786440 | tf_op jit(solution)/shard_map/ppermute | solution.py:92
  115.9 15.3 %collective-permute-start.40 = (bf16[128,1024]{1,0:T(8,128)(2,1)}, bf16[128,1024]{1,0:T(8,128)(2,1)}, u32[]{:S(2)}, u32[]{:S(2)}) collective-permute-start(bf16[128,1024]{1,0:T(8,128)(2,1)} %collective-permute-done.39), channel_id=1, source_target_pairs={{0,1},{1,0},{2,3},{3,2},{4,5},{5,4},{6,7},{7,6},{8,9},{9,8},{10,11... | collective-permute-start | bytes 786440 | tf_op jit(solution)/shard_map/ppermute | solution.py:91
  142.1 39.0 %collective-permute-start.45 = (bf16[768,1024]{1,0:T(8,128)(2,1)S(1)}, bf16[768,1024]{1,0:T(8,128)(2,1)S(1)}, u32[]{:S(2)}, u32[]{:S(2)}) collective-permute-start(bf16[768,1024]{1,0:T(8,128)(2,1)S(1)} %convolution_add_fusion), channel_id=1, source_target_pairs={{0,1},{1,0},{2,3},{3,2},{4,5},{5,4},{6,7},{7,6},{8,9},{9,8},{10,11... | collective-permute-start | bytes 4718600 | tf_op jit(solution)/shard_map/ppermute | solution.py:113
  143.7 18.9 %collective-permute-start.47 = (bf16[192,1024]{1,0:T(8,128)(2,1)S(1)}, bf16[192,1024]{1,0:T(8,128)(2,1)S(1)}, u32[]{:S(2)}, u32[]{:S(2)}) collective-permute-start(bf16[192,1024]{1,0:T(8,128)(2,1)S(1)} %get-tuple-element.308), channel_id=1, source_target_pairs={{0,2},{1,3},{2,0},{3,1},{4,6},{5,7},{6,4},{7,5},{8,10},{9,11},{10,... | collective-permute-start | bytes 1179656 | tf_op jit(solution)/shard_map/ppermute | solution.py:110
  144.2 26.8 %collective-permute-start.48 = (bf16[192,1024]{1,0:T(8,128)(2,1)S(1)}, bf16[192,1024]{1,0:T(8,128)(2,1)S(1)}, u32[]{:S(2)}, u32[]{:S(2)}) collective-permute-start(bf16[192,1024]{1,0:T(8,128)(2,1)S(1)} %get-tuple-element.307), channel_id=1, source_target_pairs={{0,2},{1,3},{2,0},{3,1},{4,6},{5,7},{6,4},{7,5},{8,10},{9,11},{10,... | collective-permute-start | bytes 1179656 | tf_op jit(solution)/shard_map/ppermute | solution.py:110
  145.8 33.2 %collective-permute-start.49 = (bf16[192,1024]{1,0:T(8,128)(2,1)S(1)}, bf16[192,1024]{1,0:T(8,128)(2,1)S(1)}, u32[]{:S(2)}, u32[]{:S(2)}) collective-permute-start(bf16[192,1024]{1,0:T(8,128)(2,1)S(1)} %get-tuple-element.306), channel_id=1, source_target_pairs={{0,2},{1,3},{2,0},{3,1},{4,6},{5,7},{6,4},{7,5},{8,10},{9,11},{10,... | collective-permute-start | bytes 1179656 | tf_op jit(solution)/shard_map/ppermute | solution.py:110
  154.2 26.7 %collective-permute-start.50 = (bf16[192,1024]{1,0:T(8,128)(2,1)S(1)}, bf16[192,1024]{1,0:T(8,128)(2,1)S(1)}, u32[]{:S(2)}, u32[]{:S(2)}) collective-permute-start(bf16[192,1024]{1,0:T(8,128)(2,1)S(1)} %collective-permute-done.46), channel_id=1, source_target_pairs={{0,1},{1,0},{2,3},{3,2},{4,5},{5,4},{6,7},{7,6},{8,9},{9,8},{10,11... | collective-permute-start | bytes 1179656 | tf_op jit(solution)/shard_map/ppermute | solution.py:112
  162.7 18.3 %collective-permute-start.51 = (bf16[192,1024]{1,0:T(8,128)(2,1)S(1)}, bf16[192,1024]{1,0:T(8,128)(2,1)S(1)}, u32[]{:S(2)}, u32[]{:S(2)}) collective-permute-start(bf16[192,1024]{1,0:T(8,128)(2,1)S(1)} %collective-permute-done.47), channel_id=1, source_target_pairs={{0,1},{1,0},{2,3},{3,2},{4,5},{5,4},{6,7},{7,6},{8,9},{9,8},{10,11... | collective-permute-start | bytes 1179656 | tf_op jit(solution)/shard_map/ppermute | solution.py:112
  196.4 14.7 %collective-permute-start.1 = (bf16[256,1024]{1,0:T(8,128)(2,1)S(1)}, bf16[256,1024]{1,0:T(8,128)(2,1)}, u32[]{:S(2)}, u32[]{:S(2)}) collective-permute-start(bf16[256,1024]{1,0:T(8,128)(2,1)S(1)} %convert_element_type.186), channel_id=1, source_target_pairs={{8,0},{16,8},{24,16},{28,24},{20,28},{12,20},{4,12},{0,4},{9,1},{1... | collective-permute-start | bytes 1572872 | tf_op jit(solution)/shard_map/while/body/eval_jaxpr/ppermute | solution.py:166
  (60 other events, 582.6 us)
where the time goes:
time: 312 us; the launch traced here: 310 us
  waiting for transfers between devices  125 us (40%)
  matrix products  80.7 us (26%)
  starting transfers between devices  62.6 us (20%)
  other arithmetic  40 us (13%)
    dot_general x8, matrix products, feat_part(): return jnp.dot(kern, w_rows, preferred_element_type=jnp.float32)  44.4 us
    ppermute x7, waiting for transfers between devices, w_step(): wb = lax.ppermute(wb, 'blk', bwd)  38.4 us
    ppermute x7, waiting for transfers between devices, r_step(): cnt_send = lax.ppermute(cnt_send, 'blk', fwd)  37.9 us
    ppermute x4, waiting for transfers between devices, per_device(): y_j = lax.ppermute(feature_cols[j * step:(j + 1) * step], 'cent', ypair)  28.7 us
    dot_general x16, matrix products, part_sums(): lax.dot_general(cols, assign, (((0,), (0,)), ((), ())), preferred_element...  26.8 us
    add x7, other arithmetic, r_step(): rbk.astype(jnp.float32) + pb  15.1 us
    ppermute x7, waiting for transfers between devices, w_step(): lb = lax.ppermute(lb, 'blk', bwd)  12.9 us
    ppermute x7, starting transfers between devices, w_step(): wb = lax.ppermute(wb, 'blk', bwd)  11.5 us
  transfers between devices with their start and end apart: 75, of which 28 were waited for; matrix products, arithmetic and copies ran while one was open for 26% of the time, Pallas kernels for 0%

commit v1 on v0

--- a/solution.py
+++ b/solution.py
@@ -161,18 +161,22 @@
             )
 
         def r_step(s, carry):
-            acc_a, acc_b, cnt_send, cnt = carry
+            acc_a, acc_b, pa, pb, cnt_send, cnt = carry
             ra = lax.ppermute(acc_a.astype(jnp.bfloat16), "blk", fwd)
             rbk = lax.ppermute(acc_b.astype(jnp.bfloat16), "blk", bwd)
             cnt_send = lax.ppermute(cnt_send, "blk", fwd)
-            pa = part_sums(ring_blk(p - 1 - s), 0)
-            pb = part_sums(ring_blk(p + 1 + s), rh)
-            return ra.astype(jnp.float32) + pa, rbk.astype(jnp.float32) + pb, cnt_send, cnt + cnt_send
+            na = part_sums(ring_blk(p - 2 - s), 0)
+            nbp = part_sums(ring_blk(p + 2 + s), rh)
+            acc_a = ra.astype(jnp.float32) + pa
+            acc_b = rbk.astype(jnp.float32) + pb
+            return acc_a, acc_b, na, nbp, cnt_send, cnt + cnt_send
 
         acc_a = part_sums(ring_blk(p - 1), 0)
         acc_b = part_sums(ring_blk(p + 1), rh)
-        acc_a, acc_b, _, counts = run_steps(
-            1, nb, r_step, (acc_a, acc_b, part_counts, part_counts), False
+        pa0 = part_sums(ring_blk(p - 2), 0)
+        pb0 = part_sums(ring_blk(p + 2), rh)
+        acc_a, acc_b, _, _, _, counts = run_steps(
+            1, nb, r_step, (acc_a, acc_b, pa0, pb0, part_counts, part_counts), False
         )
         sums = jnp.concatenate([acc_a, acc_b], axis=0)
         return (assign, sums / jnp.maximum(counts, 1.0)[None, :])

time: 312 us -> 350 us (1.12)
  matrix products: 80.7 us -> 98.4 us
  waiting for transfers between devices: 125 us -> 134 us
  local copies, waits for them, and re-layouts: 0.64 us -> 7.01 us
  starting transfers between devices: 62.6 us -> 66.8 us
    dot_general x16 -> x18, matrix products: 26.8 us -> 44.3 us  [part_sums(): lax.dot_general(cols, assign, (((0,), (0,)), ((), ())), preferred_element...]
    ppermute x7, waiting for transfers between devices: 37.9 us -> 47.9 us  [r_step(): cnt_send = lax.ppermute(cnt_send, 'blk', fwd)]
    convert_element_type x7, other arithmetic: 0.49 us -> 6.08 us  [r_step(): rbk = lax.ppermute(acc_b.astype(jnp.bfloat16), 'blk', bwd)]
    while x21 -> x49, local copies, waits for them, and re-layouts: 0.04 us -> 5.62 us
    add x21, other arithmetic: 23.6 us -> 18.2 us  [the longest x7 10.4 us: r_step(): acc_a = ra.astype(jnp.float32) + pa]
    ppermute x7, starting transfers between devices: 10.6 us -> 5.45 us  [r_step(): rbk = lax.ppermute(acc_b.astype(jnp.bfloat16), 'blk', bwd)]
    ppermute x7, starting transfers between devices: 3.93 us -> 8.74 us  [r_step(): cnt_send = lax.ppermute(cnt_send, 'blk', fwd)]
    ppermute x7, starting transfers between devices: 4.66 us -> 9.04 us  [r_step(): ra = lax.ppermute(acc_a.astype(jnp.bfloat16), 'blk', fwd)]
  transfers between devices with their start and end apart: 75 -> 75, of which waited for: 28 -> 28; matrix products, arithmetic and copies ran while one was open for 26% -> 24% of each run, Pallas kernels for 0% -> 0%
where the time goes in v1:
time: 350 us; the launch traced here: 348 us
  waiting for transfers between devices  134 us (38%)
  matrix products  98.4 us (28%)
  starting transfers between devices  66.8 us (19%)
  other arithmetic  40.5 us (12%)
  local copies, waits for them, and re-layouts  7.01 us (2%)
    ppermute x7, waiting for transfers between devices, r_step(): cnt_send = lax.ppermute(cnt_send, 'blk', fwd)  47.9 us
    dot_general x8, matrix products, feat_part(): return jnp.dot(kern, w_rows, preferred_element_type=jnp.float32)  44.5 us
    dot_general x18, matrix products, part_sums(): lax.dot_general(cols, assign, (((0,), (0,)), ((), ())), preferred_element...  44.3 us
    ppermute x7, waiting for transfers between devices, w_step(): wb = lax.ppermute(wb, 'blk', bwd)  38.6 us
    ppermute x4, waiting for transfers between devices, per_device(): y_j = lax.ppermute(feature_cols[j * step:(j + 1) * step], 'cent', ypair)  28.7 us
    ppermute x7, waiting for transfers between devices, w_step(): lb = lax.ppermute(lb, 'blk', bwd)  12.9 us
    ppermute x7, starting transfers between devices, w_step(): wb = lax.ppermute(wb, 'blk', bwd)  11.7 us
    add x7, other arithmetic, r_step(): acc_a = ra.astype(jnp.float32) + pa  10.4 us
  transfers between devices with their start and end apart: 75, of which 28 were waited for; matrix products, arithmetic and copies ran while one was open for 24% of the time, Pallas kernels for 0%

profile of v1, /device:TPU:0, one launch (start us, length us, event | category | flops | bytes accessed | tf_op | source)
XLA Modules:
  0.0 348.4 jit_solution(10994881331766523234)
XLA Ops:
  3.8 3.0 collective-permute-start.5
  9.4 4.8 %collective-permute-done.5 = bf16[128,1024]{1,0:T(8,128)(2,1)} collective-permute-done((bf16[128,1024]{1,0:T(8,128)(2,1)S(1)}, bf16[128,1024]{1,0:T(8,128)(2,1)}, u32[]{:S(2)}, u32[]{:S(2)}) %collective-permute-start.5) | collective-permute-done | bytes 262176 | tf_op jit(solution)/shard_map/ppermute | solution.py:90
  18.7 6.7 %collective-permute-done.8 = bf16[256,1024]{1,0:T(8,128)(2,1)} collective-permute-done((bf16[256,1024]{1,0:T(8,128)(2,1)S(1)}, bf16[256,1024]{1,0:T(8,128)(2,1)}, u32[]{:S(2)}, u32[]{:S(2)}) %collective-permute-start.8) | collective-permute-done | bytes 524320 | tf_op jit(solution)/shard_map/ppermute | solution.py:88
  27.3 3.6 %collective-permute-done.11 = bf16[128,1024]{1,0:T(8,128)(2,1)S(1)} collective-permute-done((bf16[128,1024]{1,0:T(8,128)(2,1)}, bf16[128,1024]{1,0:T(8,128)(2,1)S(1)}, u32[]{:S(2)}, u32[]{:S(2)}) %collective-permute-start.11) | collective-permute-done | bytes 262176 | tf_op jit(solution)/shard_map/ppermute | solution.py:90
  36.2 4.9 %fusion.118 = f32[768,1024]{1,0:T(8,128)} fusion(bf16[512,1024]{1,0:T(8,128)(2,1)S(1)} %copy-done.5, bf16[512,1024]{1,0:T(8,128)(2,1)S(1)} %fusion.9, bf16[768,1024]{1,0:T(8,128)(2,1)} %param.6, f32[768]{0:T(1024)S(1)} %add_rsqrt_fusion), kind=kOutput, calls=%fused_computation.115 | convolution fusion | flops 1613758464 | bytes 6818816 | tf_op jit(solution)/shard_map/dot_general | solution.py:75
  42.7 4.3 %collective-permute-done.17 = bf16[128,1024]{1,0:T(8,128)(2,1)} collective-permute-done((bf16[128,1024]{1,0:T(8,128)(2,1)S(1)}, bf16[128,1024]{1,0:T(8,128)(2,1)}, u32[]{:S(2)}, u32[]{:S(2)}) %collective-permute-start.17) | collective-permute-done | bytes 262176 | tf_op jit(solution)/shard_map/ppermute | solution.py:90
  49.3 6.5 %convolution_add_fusion.6 = f32[768,1024]{1,0:T(8,128)} fusion(f32[768,1024]{1,0:T(8,128)} %fusion.118, bf16[128,1024]{1,0:T(8,128)(2,1)} %copy-done.9, bf16[128,1024]{1,0:T(8,128)(2,1)} %collective-permute-done.5, bf16[128,1024]{1,0:T(8,128)(2,1)} %copy-done.10, bf16[128,1024]{1,0:T(8,128)(2,1)} %collective-permute-done.3, ...), kind=kOutput, calls=%fused_computation.36 | convolution fusion | flops 1620836352 | bytes 9964544 | tf_op jit(solution)/shard_map/dot_general | solution.py:75
  61.1 5.8 %convolution_add_fusion.5 = f32[768,1024]{1,0:T(8,128)} fusion(f32[768,1024]{1,0:T(8,128)} %convolution_add_fusion.6, bf16[128,1024]{1,0:T(8,128)(2,1)} %collective-permute-done.12, bf16[128,1024]{1,0:T(8,128)(2,1)S(1)} %collective-permute-done.11, bf16[128,1024]{1,0:T(8,128)(2,1)} %collective-permute-done.10, ...), kind=kOutput, calls=%fused_computation.35 | convolution fusion | flops 1620836352 | bytes 9964544 | tf_op jit(solution)/shard_map/dot_general | solution.py:75
  69.2 7.6 %collective-permute-done.20 = bf16[256,1024]{1,0:T(8,128)(2,1)S(1)} collective-permute-done((bf16[256,1024]{1,0:T(8,128)(2,1)}, bf16[256,1024]{1,0:T(8,128)(2,1)S(1)}, u32[]{:S(2)}, u32[]{:S(2)}) %collective-permute-start.20) | collective-permute-done | bytes 524320 | tf_op jit(solution)/shard_map/ppermute | solution.py:88
  78.8 5.7 %convolution_add_fusion.4 = f32[768,1024]{1,0:T(8,128)} fusion(f32[768,1024]{1,0:T(8,128)} %convolution_add_fusion.5, bf16[128,1024]{1,0:T(8,128)(2,1)} %copy-done.11, bf16[128,1024]{1,0:T(8,128)(2,1)} %collective-permute-done.17, bf16[128,1024]{1,0:T(8,128)(2,1)} %collective-permute-done.16, bf16[128,1024]{1,0:T(8,128)(2,1)} %collective-permute-done.15, ...), kind=kOutput, calls=%fused_computation.34 | convolution fusion | flops 1620836352 | bytes 9964544 | tf_op jit(solution)/shard_map/dot_general | solution.py:75
  86.4 6.8 %collective-permute-done.26 = bf16[256,1024]{1,0:T(8,128)(2,1)} collective-permute-done((bf16[256,1024]{1,0:T(8,128)(2,1)S(1)}, bf16[256,1024]{1,0:T(8,128)(2,1)}, u32[]{:S(2)}, u32[]{:S(2)}) %collective-permute-start.26) | collective-permute-done | bytes 524320 | tf_op jit(solution)/shard_map/ppermute | solution.py:88
  95.2 5.9 %convolution_add_fusion.3 = f32[768,1024]{1,0:T(8,128)} fusion(f32[768,1024]{1,0:T(8,128)} %convolution_add_fusion.4, bf16[128,1024]{1,0:T(8,128)(2,1)} %collective-permute-done.24, bf16[128,1024]{1,0:T(8,128)(2,1)} %collective-permute-done.23, bf16[128,1024]{1,0:T(8,128)(2,1)} %collective-permute-done.22, bf16[128,1024]{1,0:T(8,128)(2,1)} %collective-permute-done.21, ...), kind=kOutput, calls=%fused_computation.33 | convolution fusion | flops 1620836352 | bytes 9964544 | tf_op jit(solution)/shard_map/dot_general | solution.py:75
  103.2 5.0 %collective-permute-done.32 = bf16[256,1024]{1,0:T(8,128)(2,1)S(1)} collective-permute-done((bf16[256,1024]{1,0:T(8,128)(2,1)}, bf16[256,1024]{1,0:T(8,128)(2,1)S(1)}, u32[]{:S(2)}, u32[]{:S(2)}) %collective-permute-start.32) | collective-permute-done | bytes 524320 | tf_op jit(solution)/shard_map/ppermute | solution.py:88
  110.2 5.7 %convolution_add_fusion.2 = f32[768,1024]{1,0:T(8,128)} fusion(f32[768,1024]{1,0:T(8,128)} %convolution_add_fusion.3, bf16[128,1024]{1,0:T(8,128)(2,1)} %collective-permute-done.30, bf16[128,1024]{1,0:T(8,128)(2,1)} %collective-permute-done.29, bf16[128,1024]{1,0:T(8,128)(2,1)} %collective-permute-done.28, bf16[128,1024]{1,0:T(8,128)(2,1)} %collective-permute-done.27, ...), kind=kOutput, calls=%fused_computation.32 | convolution fusion | flops 1620836352 | bytes 9964544 | tf_op jit(solution)/shard_map/dot_general | solution.py:75
  116.4 7.4 %collective-permute-done.38 = bf16[256,1024]{1,0:T(8,128)(2,1)} collective-permute-done((bf16[256,1024]{1,0:T(8,128)(2,1)S(1)}, bf16[256,1024]{1,0:T(8,128)(2,1)}, u32[]{:S(2)}, u32[]{:S(2)}) %collective-permute-start.38) | collective-permute-done | bytes 524320 | tf_op jit(solution)/shard_map/ppermute | solution.py:88
  125.9 5.8 %convolution_add_fusion.1 = f32[768,1024]{1,0:T(8,128)} fusion(f32[768,1024]{1,0:T(8,128)} %convolution_add_fusion.2, bf16[128,1024]{1,0:T(8,128)(2,1)} %collective-permute-done.36, bf16[128,1024]{1,0:T(8,128)(2,1)S(1)} %collective-permute-done.35, bf16[128,1024]{1,0:T(8,128)(2,1)} %collective-permute-done.34, ...), kind=kOutput, calls=%fused_computation.31 | convolution fusion | flops 1620836352 | bytes 9964544 | tf_op jit(solution)/shard_map/dot_general | solution.py:75
  131.7 5.0 %collective-permute-done.44 = bf16[256,1024]{1,0:T(8,128)(2,1)S(1)} collective-permute-done((bf16[256,1024]{1,0:T(8,128)(2,1)}, bf16[256,1024]{1,0:T(8,128)(2,1)S(1)}, u32[]{:S(2)}, u32[]{:S(2)}) %collective-permute-start.44) | collective-permute-done | bytes 524320 | tf_op jit(solution)/shard_map/ppermute | solution.py:88
  137.9 4.4 %convolution_add_fusion = bf16[768,1024]{1,0:T(8,128)(2,1)S(1)} fusion(f32[768,1024]{1,0:T(8,128)} %convolution_add_fusion.1, bf16[128,1024]{1,0:T(8,128)(2,1)} %collective-permute-done.42, bf16[128,1024]{1,0:T(8,128)(2,1)} %collective-permute-done.41, bf16[128,1024]{1,0:T(8,128)(2,1)} %collective-permute-done.40, ...), kind=kOutput, calls=%fused_computation.30 | convolution fusion | flops 1621622784 | bytes 8391680 | tf_op jit(solution)/shard_map/dot_general | solution.py:75
  146.7 3.7 %fusion.16 = f32[768,1024]{1,0:T(8,128)S(1)} fusion(bf16[768,1024]{1,0:T(8,128)(2,1)S(1)} %convolution_add_fusion, bf16[1024,4096]{1,0:T(8,128)(2,1)} %param.9, s32[]{:T(128)S(6)} %select_n.249), kind=kOutput, calls=%fused_computation.28 | convolution fusion | flops 1610612736 | bytes 6815748 | tf_op jit(solution)/shard_map/dot_general | solution.py:125
  150.4 4.3 %collective-permute-done.46 = bf16[192,1024]{1,0:T(8,128)(2,1)S(1)} collective-permute-done((bf16[192,1024]{1,0:T(8,128)(2,1)S(1)}, bf16[192,1024]{1,0:T(8,128)(2,1)S(1)}, u32[]{:S(2)}, u32[]{:S(2)}) %collective-permute-start.46) | collective-permute-done | bytes 393248 | tf_op jit(solution)/shard_map/ppermute | solution.py:110
  154.7 8.3 %collective-permute-done.47 = bf16[192,1024]{1,0:T(8,128)(2,1)S(1)} collective-permute-done((bf16[192,1024]{1,0:T(8,128)(2,1)S(1)}, bf16[192,1024]{1,0:T(8,128)(2,1)S(1)}, u32[]{:S(2)}, u32[]{:S(2)}) %collective-permute-start.47) | collective-permute-done | bytes 393248 | tf_op jit(solution)/shard_map/ppermute | solution.py:110
  163.2 8.3 %collective-permute-done.48 = bf16[192,1024]{1,0:T(8,128)(2,1)S(1)} collective-permute-done((bf16[192,1024]{1,0:T(8,128)(2,1)S(1)}, bf16[192,1024]{1,0:T(8,128)(2,1)S(1)}, u32[]{:S(2)}, u32[]{:S(2)}) %collective-permute-start.48) | collective-permute-done | bytes 393248 | tf_op jit(solution)/shard_map/ppermute | solution.py:110
  171.6 7.8 %collective-permute-done.49 = bf16[192,1024]{1,0:T(8,128)(2,1)S(1)} collective-permute-done((bf16[192,1024]{1,0:T(8,128)(2,1)S(1)}, bf16[192,1024]{1,0:T(8,128)(2,1)S(1)}, u32[]{:S(2)}, u32[]{:S(2)}) %collective-permute-start.49) | collective-permute-done | bytes 393248 | tf_op jit(solution)/shard_map/ppermute | solution.py:110
  198.6 146.3 %while.26 = (s32[]{:T(128)}, f32[256,1024]{1,0:T(8,128)S(1)}, f32[256,1024]{1,0:T(8,128)}, f32[256,1024]{1,0:T(8,128)}, f32[256,1024]{1,0:T(8,128)}, /*index=5*/...) while((s32[]{:T(128)}, f32[256,1024]{1,0:T(8,128)S(1)}, ...), condition=%wide.region_6.7_spmd, body=%wide.region_5.6_spmd.sunk | while | flops 806880256 | bytes 29136180 | solution.py:28
  203.7 9.2 %collective-permute-done.2 = f32[1024]{0:T(1024)S(1)} collective-permute-done((f32[1024]{0:T(1024)S(1)}, f32[1024]{0:T(1024)S(1)}, u32[]{:S(2)}, u32[]{:S(2)}) %collective-permute-start.2) | collective-permute-done | bytes 4128 | tf_op jit(solution)/shard_map/while/body/eval_jaxpr/ppermute | solution.py:167
  226.9 8.4 %collective-permute-done.2 = f32[1024]{0:T(1024)S(1)} collective-permute-done((f32[1024]{0:T(1024)S(1)}, f32[1024]{0:T(1024)S(1)}, u32[]{:S(2)}, u32[]{:S(2)}) %collective-permute-start.2) | collective-permute-done | bytes 4128 | tf_op jit(solution)/shard_map/while/body/eval_jaxpr/ppermute | solution.py:167
  249.3 7.5 %collective-permute-done.2 = f32[1024]{0:T(1024)S(1)} collective-permute-done((f32[1024]{0:T(1024)S(1)}, f32[1024]{0:T(1024)S(1)}, u32[]{:S(2)}, u32[]{:S(2)}) %collective-permute-start.2) | collective-permute-done | bytes 4128 | tf_op jit(solution)/shard_map/while/body/eval_jaxpr/ppermute | solution.py:167
  270.9 6.6 %collective-permute-done.2 = f32[1024]{0:T(1024)S(1)} collective-permute-done((f32[1024]{0:T(1024)S(1)}, f32[1024]{0:T(1024)S(1)}, u32[]{:S(2)}, u32[]{:S(2)}) %collective-permute-start.2) | collective-permute-done | bytes 4128 | tf_op jit(solution)/shard_map/while/body/eval_jaxpr/ppermute | solution.py:167
  291.6 5.7 %collective-permute-done.2 = f32[1024]{0:T(1024)S(1)} collective-permute-done((f32[1024]{0:T(1024)S(1)}, f32[1024]{0:T(1024)S(1)}, u32[]{:S(2)}, u32[]{:S(2)}) %collective-permute-start.2) | collective-permute-done | bytes 4128 | tf_op jit(solution)/shard_map/while/body/eval_jaxpr/ppermute | solution.py:167
  311.4 5.2 %collective-permute-done.2 = f32[1024]{0:T(1024)S(1)} collective-permute-done((f32[1024]{0:T(1024)S(1)}, f32[1024]{0:T(1024)S(1)}, u32[]{:S(2)}, u32[]{:S(2)}) %collective-permute-start.2) | collective-permute-done | bytes 4128 | tf_op jit(solution)/shard_map/while/body/eval_jaxpr/ppermute | solution.py:167
  330.7 5.2 %collective-permute-done.2 = f32[1024]{0:T(1024)S(1)} collective-permute-done((f32[1024]{0:T(1024)S(1)}, f32[1024]{0:T(1024)S(1)}, u32[]{:S(2)}, u32[]{:S(2)}) %collective-permute-start.2) | collective-permute-done | bytes 4128 | tf_op jit(solution)/shard_map/while/body/eval_jaxpr/ppermute | solution.py:167
  344.9 3.5 maximum_divide_fusion
  (286 shorter events, 164.7 us)
Async XLA Ops:
  7.3 18.1 %collective-permute-start.8 = (bf16[256,1024]{1,0:T(8,128)(2,1)S(1)}, bf16[256,1024]{1,0:T(8,128)(2,1)}, u32[]{:S(2)}, u32[]{:S(2)}) collective-permute-start(bf16[256,1024]{1,0:T(8,128)(2,1)S(1)} %get-tuple-element.365), channel_id=1, source_target_pairs={{8,0},{16,8},{24,16},{28,24},{20,28},{12,20},{4,12},{0,4},{9,1},{1... | collective-permute-start | bytes 1572872 | tf_op jit(solution)/shard_map/ppermute | solution.py:88
  14.2 20.3 %collective-permute-start.7 = (bf16[256,1024]{1,0:T(8,128)(2,1)S(1)}, bf16[256,1024]{1,0:T(8,128)(2,1)}, u32[]{:S(2)}, u32[]{:S(2)}) collective-permute-start(bf16[256,1024]{1,0:T(8,128)(2,1)S(1)} %get-tuple-element.364), channel_id=1, source_target_pairs={{0,8},{8,16},{16,24},{24,28},{28,20},{20,12},{12,4},{4,0},{1,9},{9... | collective-permute-start | bytes 1572872 | tf_op jit(solution)/shard_map/ppermute | solution.py:87
  16.5 17.9 %collective-permute-start.9 = (bf16[128,1024]{1,0:T(8,128)(2,1)}, bf16[128,1024]{1,0:T(8,128)(2,1)}, u32[]{:S(2)}, u32[]{:S(2)}) collective-permute-start(bf16[128,1024]{1,0:T(8,128)(2,1)} %collective-permute-done.3), channel_id=1, source_target_pairs={{0,8},{8,16},{16,24},{24,28},{28,20},{20,12},{12,4},{4,0},{1,9},{9... | collective-permute-start | bytes 786440 | tf_op jit(solution)/shard_map/ppermute | solution.py:89
  25.4 23.5 %collective-permute-start.14 = (bf16[256,1024]{1,0:T(8,128)(2,1)}, bf16[256,1024]{1,0:T(8,128)(2,1)}, u32[]{:S(2)}, u32[]{:S(2)}) collective-permute-start(bf16[256,1024]{1,0:T(8,128)(2,1)} %collective-permute-done.8), channel_id=1, source_target_pairs={{8,0},{16,8},{24,16},{28,24},{20,28},{12,20},{4,12},{0,4},{9,1},{1... | collective-permute-start | bytes 1572872 | tf_op jit(solution)/shard_map/ppermute | solution.py:88
  30.9 16.1 %collective-permute-start.17 = (bf16[128,1024]{1,0:T(8,128)(2,1)S(1)}, bf16[128,1024]{1,0:T(8,128)(2,1)}, u32[]{:S(2)}, u32[]{:S(2)}) collective-permute-start(bf16[128,1024]{1,0:T(8,128)(2,1)S(1)} %collective-permute-done.11), channel_id=1, source_target_pairs={{8,0},{16,8},{24,16},{28,24},{20,28},{12,20},{4,12},{0,4},{9,1},{1... | collective-permute-start | bytes 786440 | tf_op jit(solution)/shard_map/ppermute | solution.py:90
  41.1 15.0 %collective-permute-start.13 = (bf16[256,1024]{1,0:T(8,128)(2,1)}, bf16[256,1024]{1,0:T(8,128)(2,1)S(1)}, u32[]{:S(2)}, u32[]{:S(2)}) collective-permute-start(bf16[256,1024]{1,0:T(8,128)(2,1)} %collective-permute-done.7), channel_id=1, source_target_pairs={{0,8},{8,16},{16,24},{24,28},{28,20},{20,12},{12,4},{4,0},{1,9},{9... | collective-permute-start | bytes 1572872 | tf_op jit(solution)/shard_map/ppermute | solution.py:87
  57.7 19.0 %collective-permute-start.20 = (bf16[256,1024]{1,0:T(8,128)(2,1)}, bf16[256,1024]{1,0:T(8,128)(2,1)S(1)}, u32[]{:S(2)}, u32[]{:S(2)}) collective-permute-start(bf16[256,1024]{1,0:T(8,128)(2,1)} %collective-permute-done.14), channel_id=1, source_target_pairs={{8,0},{16,8},{24,16},{28,24},{20,28},{12,20},{4,12},{0,4},{9,1},{1... | collective-permute-start | bytes 1572872 | tf_op jit(solution)/shard_map/ppermute | solution.py:88
  59.3 19.0 %collective-permute-start.19 = (bf16[256,1024]{1,0:T(8,128)(2,1)S(1)}, bf16[256,1024]{1,0:T(8,128)(2,1)S(1)}, u32[]{:S(2)}, u32[]{:S(2)}) collective-permute-start(bf16[256,1024]{1,0:T(8,128)(2,1)S(1)} %collective-permute-done.13), channel_id=1, source_target_pairs={{0,8},{8,16},{16,24},{24,28},{28,20},{20,12},{12,4},{4,0},{1,9},{9... | collective-permute-start | bytes 1572872 | tf_op jit(solution)/shard_map/ppermute | solution.py:87
  66.9 17.6 %collective-permute-start.27 = (bf16[128,1024]{1,0:T(8,128)(2,1)}, bf16[128,1024]{1,0:T(8,128)(2,1)}, u32[]{:S(2)}, u32[]{:S(2)}) collective-permute-start(bf16[128,1024]{1,0:T(8,128)(2,1)} %collective-permute-done.21), channel_id=1, source_target_pairs={{0,8},{8,16},{16,24},{24,28},{28,20},{20,12},{12,4},{4,0},{1,9},{9... | collective-permute-start | bytes 786440 | tf_op jit(solution)/shard_map/ppermute | solution.py:89
  68.8 15.7 %collective-permute-start.30 = (bf16[128,1024]{1,0:T(8,128)(2,1)}, bf16[128,1024]{1,0:T(8,128)(2,1)}, u32[]{:S(2)}, u32[]{:S(2)}) collective-permute-start(bf16[128,1024]{1,0:T(8,128)(2,1)} %collective-permute-done.29), channel_id=1, source_target_pairs={{0,1},{1,0},{2,3},{3,2},{4,5},{5,4},{6,7},{7,6},{8,9},{9,8},{10,11... | collective-permute-start | bytes 786440 | tf_op jit(solution)/shard_map/ppermute | solution.py:92
  69.0 17.2 %collective-permute-start.35 = (bf16[128,1024]{1,0:T(8,128)(2,1)}, bf16[128,1024]{1,0:T(8,128)(2,1)S(1)}, u32[]{:S(2)}, u32[]{:S(2)}) collective-permute-start(bf16[128,1024]{1,0:T(8,128)(2,1)} %collective-permute-done.29), channel_id=1, source_target_pairs={{8,0},{16,8},{24,16},{28,24},{20,28},{12,20},{4,12},{0,4},{9,1},{1... | collective-permute-start | bytes 786440 | tf_op jit(solution)/shard_map/ppermute | solution.py:90
  76.8 16.4 %collective-permute-start.26 = (bf16[256,1024]{1,0:T(8,128)(2,1)S(1)}, bf16[256,1024]{1,0:T(8,128)(2,1)}, u32[]{:S(2)}, u32[]{:S(2)}) collective-permute-start(bf16[256,1024]{1,0:T(8,128)(2,1)S(1)} %collective-permute-done.20), channel_id=1, source_target_pairs={{8,0},{16,8},{24,16},{28,24},{20,28},{12,20},{4,12},{0,4},{9,1},{1... | collective-permute-start | bytes 1572872 | tf_op jit(solution)/shard_map/ppermute | solution.py:88
  78.3 16.5 %collective-permute-start.25 = (bf16[256,1024]{1,0:T(8,128)(2,1)S(1)}, bf16[256,1024]{1,0:T(8,128)(2,1)S(1)}, u32[]{:S(2)}, u32[]{:S(2)}) collective-permute-start(bf16[256,1024]{1,0:T(8,128)(2,1)S(1)} %collective-permute-done.19), channel_id=1, source_target_pairs={{0,8},{8,16},{16,24},{24,28},{28,20},{20,12},{12,4},{4,0},{1,9},{9... | collective-permute-start | bytes 1572872 | tf_op jit(solution)/shard_map/ppermute | solution.py:87
  84.5 16.6 %collective-permute-start.28 = (bf16[128,1024]{1,0:T(8,128)(2,1)}, bf16[128,1024]{1,0:T(8,128)(2,1)}, u32[]{:S(2)}, u32[]{:S(2)}) collective-permute-start(bf16[128,1024]{1,0:T(8,128)(2,1)} %collective-permute-done.27), channel_id=1, source_target_pairs={{0,1},{1,0},{2,3},{3,2},{4,5},{5,4},{6,7},{7,6},{8,9},{9,8},{10,11... | collective-permute-start | bytes 786440 | tf_op jit(solution)/shard_map/ppermute | solution.py:91
  84.5 18.2 %collective-permute-start.33 = (bf16[128,1024]{1,0:T(8,128)(2,1)}, bf16[128,1024]{1,0:T(8,128)(2,1)}, u32[]{:S(2)}, u32[]{:S(2)}) collective-permute-start(bf16[128,1024]{1,0:T(8,128)(2,1)} %collective-permute-done.27), channel_id=1, source_target_pairs={{0,8},{8,16},{16,24},{24,28},{28,20},{20,12},{12,4},{4,0},{1,9},{9... | collective-permute-start | bytes 786440 | tf_op jit(solution)/shard_map/ppermute | solution.py:89
  86.2 16.5 %collective-permute-start.36 = (bf16[128,1024]{1,0:T(8,128)(2,1)S(1)}, bf16[128,1024]{1,0:T(8,128)(2,1)}, u32[]{:S(2)}, u32[]{:S(2)}) collective-permute-start(bf16[128,1024]{1,0:T(8,128)(2,1)S(1)} %collective-permute-done.35), channel_id=1, source_target_pairs={{0,1},{1,0},{2,3},{3,2},{4,5},{5,4},{6,7},{7,6},{8,9},{9,8},{10,11... | collective-permute-start | bytes 786440 | tf_op jit(solution)/shard_map/ppermute | solution.py:92
  93.2 15.0 %collective-permute-start.32 = (bf16[256,1024]{1,0:T(8,128)(2,1)}, bf16[256,1024]{1,0:T(8,128)(2,1)S(1)}, u32[]{:S(2)}, u32[]{:S(2)}) collective-permute-start(bf16[256,1024]{1,0:T(8,128)(2,1)} %collective-permute-done.26), channel_id=1, source_target_pairs={{8,0},{16,8},{24,16},{28,24},{20,28},{12,20},{4,12},{0,4},{9,1},{1... | collective-permute-start | bytes 1572872 | tf_op jit(solution)/shard_map/ppermute | solution.py:88
  94.8 15.0 %collective-permute-start.31 = (bf16[256,1024]{1,0:T(8,128)(2,1)S(1)}, bf16[256,1024]{1,0:T(8,128)(2,1)S(1)}, u32[]{:S(2)}, u32[]{:S(2)}) collective-permute-start(bf16[256,1024]{1,0:T(8,128)(2,1)S(1)} %collective-permute-done.25), channel_id=1, source_target_pairs={{0,8},{8,16},{16,24},{24,28},{28,20},{20,12},{12,4},{4,0},{1,9},{9... | collective-permute-start | bytes 1572872 | tf_op jit(solution)/shard_map/ppermute | solution.py:87
  101.1 14.8 %collective-permute-start.41 = (bf16[128,1024]{1,0:T(8,128)(2,1)S(1)}, bf16[128,1024]{1,0:T(8,128)(2,1)}, u32[]{:S(2)}, u32[]{:S(2)}) collective-permute-start(bf16[128,1024]{1,0:T(8,128)(2,1)S(1)} %collective-permute-done.35), channel_id=1, source_target_pairs={{8,0},{16,8},{24,16},{28,24},{20,28},{12,20},{4,12},{0,4},{9,1},{1... | collective-permute-start | bytes 786440 | tf_op jit(solution)/shard_map/ppermute | solution.py:90
  102.7 23.1 %collective-permute-start.34 = (bf16[128,1024]{1,0:T(8,128)(2,1)}, bf16[128,1024]{1,0:T(8,128)(2,1)}, u32[]{:S(2)}, u32[]{:S(2)}) collective-permute-start(bf16[128,1024]{1,0:T(8,128)(2,1)} %collective-permute-done.33), channel_id=1, source_target_pairs={{0,1},{1,0},{2,3},{3,2},{4,5},{5,4},{6,7},{7,6},{8,9},{9,8},{10,11... | collective-permute-start | bytes 786440 | tf_op jit(solution)/shard_map/ppermute | solution.py:91
  108.2 15.6 %collective-permute-start.38 = (bf16[256,1024]{1,0:T(8,128)(2,1)S(1)}, bf16[256,1024]{1,0:T(8,128)(2,1)}, u32[]{:S(2)}, u32[]{:S(2)}) collective-permute-start(bf16[256,1024]{1,0:T(8,128)(2,1)S(1)} %collective-permute-done.32), channel_id=1, source_target_pairs={{8,0},{16,8},{24,16},{28,24},{20,28},{12,20},{4,12},{0,4},{9,1},{1... | collective-permute-start | bytes 1572872 | tf_op jit(solution)/shard_map/ppermute | solution.py:88
  109.8 15.6 %collective-permute-start.37 = (bf16[256,1024]{1,0:T(8,128)(2,1)S(1)}, bf16[256,1024]{1,0:T(8,128)(2,1)S(1)}, u32[]{:S(2)}, u32[]{:S(2)}) collective-permute-start(bf16[256,1024]{1,0:T(8,128)(2,1)S(1)} %collective-permute-done.31), channel_id=1, source_target_pairs={{0,8},{8,16},{16,24},{24,28},{28,20},{20,12},{12,4},{4,0},{1,9},{9... | collective-permute-start | bytes 1572872 | tf_op jit(solution)/shard_map/ppermute | solution.py:87
  115.9 15.7 %collective-permute-start.42 = (bf16[128,1024]{1,0:T(8,128)(2,1)}, bf16[128,1024]{1,0:T(8,128)(2,1)}, u32[]{:S(2)}, u32[]{:S(2)}) collective-permute-start(bf16[128,1024]{1,0:T(8,128)(2,1)} %collective-permute-done.41), channel_id=1, source_target_pairs={{0,1},{1,0},{2,3},{3,2},{4,5},{5,4},{6,7},{7,6},{8,9},{9,8},{10,11... | collective-permute-start | bytes 786440 | tf_op jit(solution)/shard_map/ppermute | solution.py:92
  115.9 15.7 %collective-permute-start.40 = (bf16[128,1024]{1,0:T(8,128)(2,1)}, bf16[128,1024]{1,0:T(8,128)(2,1)}, u32[]{:S(2)}, u32[]{:S(2)}) collective-permute-start(bf16[128,1024]{1,0:T(8,128)(2,1)} %collective-permute-done.39), channel_id=1, source_target_pairs={{0,1},{1,0},{2,3},{3,2},{4,5},{5,4},{6,7},{7,6},{8,9},{9,8},{10,11... | collective-permute-start | bytes 786440 | tf_op jit(solution)/shard_map/ppermute | solution.py:91
  142.5 39.0 %collective-permute-start.45 = (bf16[768,1024]{1,0:T(8,128)(2,1)S(1)}, bf16[768,1024]{1,0:T(8,128)(2,1)S(1)}, u32[]{:S(2)}, u32[]{:S(2)}) collective-permute-start(bf16[768,1024]{1,0:T(8,128)(2,1)S(1)} %convolution_add_fusion), channel_id=1, source_target_pairs={{0,1},{1,0},{2,3},{3,2},{4,5},{5,4},{6,7},{7,6},{8,9},{9,8},{10,11... | collective-permute-start | bytes 4718600 | tf_op jit(solution)/shard_map/ppermute | solution.py:113
  144.2 18.9 %collective-permute-start.47 = (bf16[192,1024]{1,0:T(8,128)(2,1)S(1)}, bf16[192,1024]{1,0:T(8,128)(2,1)S(1)}, u32[]{:S(2)}, u32[]{:S(2)}) collective-permute-start(bf16[192,1024]{1,0:T(8,128)(2,1)S(1)} %get-tuple-element.362), channel_id=1, source_target_pairs={{0,2},{1,3},{2,0},{3,1},{4,6},{5,7},{6,4},{7,5},{8,10},{9,11},{10,... | collective-permute-start | bytes 1179656 | tf_op jit(solution)/shard_map/ppermute | solution.py:110
  144.7 26.8 %collective-permute-start.48 = (bf16[192,1024]{1,0:T(8,128)(2,1)S(1)}, bf16[192,1024]{1,0:T(8,128)(2,1)S(1)}, u32[]{:S(2)}, u32[]{:S(2)}) collective-permute-start(bf16[192,1024]{1,0:T(8,128)(2,1)S(1)} %get-tuple-element.361), channel_id=1, source_target_pairs={{0,2},{1,3},{2,0},{3,1},{4,6},{5,7},{6,4},{7,5},{8,10},{9,11},{10,... | collective-permute-start | bytes 1179656 | tf_op jit(solution)/shard_map/ppermute | solution.py:110
  146.2 33.2 %collective-permute-start.49 = (bf16[192,1024]{1,0:T(8,128)(2,1)S(1)}, bf16[192,1024]{1,0:T(8,128)(2,1)S(1)}, u32[]{:S(2)}, u32[]{:S(2)}) collective-permute-start(bf16[192,1024]{1,0:T(8,128)(2,1)S(1)} %get-tuple-element.360), channel_id=1, source_target_pairs={{0,2},{1,3},{2,0},{3,1},{4,6},{5,7},{6,4},{7,5},{8,10},{9,11},{10,... | collective-permute-start | bytes 1179656 | tf_op jit(solution)/shard_map/ppermute | solution.py:110
  154.7 26.7 %collective-permute-start.50 = (bf16[192,1024]{1,0:T(8,128)(2,1)S(1)}, bf16[192,1024]{1,0:T(8,128)(2,1)S(1)}, u32[]{:S(2)}, u32[]{:S(2)}) collective-permute-start(bf16[192,1024]{1,0:T(8,128)(2,1)S(1)} %collective-permute-done.46), channel_id=1, source_target_pairs={{0,1},{1,0},{2,3},{3,2},{4,5},{5,4},{6,7},{7,6},{8,9},{9,8},{10,11... | collective-permute-start | bytes 1179656 | tf_op jit(solution)/shard_map/ppermute | solution.py:112
  163.1 18.3 %collective-permute-start.51 = (bf16[192,1024]{1,0:T(8,128)(2,1)S(1)}, bf16[192,1024]{1,0:T(8,128)(2,1)S(1)}, u32[]{:S(2)}, u32[]{:S(2)}) collective-permute-start(bf16[192,1024]{1,0:T(8,128)(2,1)S(1)} %collective-permute-done.47), channel_id=1, source_target_pairs={{0,1},{1,0},{2,3},{3,2},{4,5},{5,4},{6,7},{7,6},{8,9},{9,8},{10,11... | collective-permute-start | bytes 1179656 | tf_op jit(solution)/shard_map/ppermute | solution.py:112
  201.6 16.4 %collective-permute-start.1 = (bf16[256,1024]{1,0:T(8,128)(2,1)}, bf16[256,1024]{1,0:T(8,128)(2,1)S(1)}, u32[]{:S(2)}, u32[]{:S(2)}) collective-permute-start(bf16[256,1024]{1,0:T(8,128)(2,1)} %convert_element_type.186), channel_id=1, source_target_pairs={{8,0},{16,8},{24,16},{28,24},{20,28},{12,20},{4,12},{0,4},{9,1},{1... | collective-permute-start | bytes 1572872 | tf_op jit(solution)/shard_map/while/body/eval_jaxpr/ppermute | solution.py:166
  224.8 15.6 %collective-permute-start.1 = (bf16[256,1024]{1,0:T(8,128)(2,1)}, bf16[256,1024]{1,0:T(8,128)(2,1)S(1)}, u32[]{:S(2)}, u32[]{:S(2)}) collective-permute-start(bf16[256,1024]{1,0:T(8,128)(2,1)} %convert_element_type.186), channel_id=1, source_target_pairs={{8,0},{16,8},{24,16},{28,24},{20,28},{12,20},{4,12},{0,4},{9,1},{1... | collective-permute-start | bytes 1572872 | tf_op jit(solution)/shard_map/while/body/eval_jaxpr/ppermute | solution.py:166
  (75 other events, 620.2 us)
